TPU v7x, 32 devices: a whole 2x2x4 slice. The times are simulated.
32 devices in a mesh: group: 2 (over y), seq: 8 (over z, x), chan: 2 (over core).
Axes of the slice: x: 2, y: 2, z: 4, core: 2. Of those that a mesh axis runs over, the one named last changes fastest.
Arguments:
- fresh: bfloat16 [2048, 3, 2048], P(('group', 'seq'), None, 'chan'), parts along dimension 0, may hold values from -6 to 6
- library: bfloat16 [8, 8, 2048], P('seq', None, 'chan'), may hold values from -6 to 6
- block_slot: int32 [8], replicated, may hold values from 0 to 7, each once
- prefix_blocks: int32 [16, 4], P('group'), parts along dimension 0, may hold values from 0 to 7, all different within a row
- short_taps: float32 [3, 3, 2048], P(None, None, 'chan'), may hold values from -4 to 4
- long_filter: float32 [1024, 2048], P('seq', 'chan'), may hold values from -2 to 2
- skip_gain: float32 [2048], P('chan'), may hold values from -6 to 6
Outputs:
- mixed: bfloat16 [2048, 2048], P(('group', 'seq'), 'chan'), parts along dimension 0
There are 2 independent parts, one for each index of `group`. A program takes and returns all parts, laid end to end along the dimension named above; an argument that names none is the same for every part. Nothing has to cross between parts.
Inputs may be any that keep to these rules, and one draw needn't show every extreme that they name: `block_slot`: each number appears once. `prefix_blocks`: every library block is named at least once; the four entries of a row differ.
All inputs are finite; a program needn't handle non-finite values.
Results may differ from a plain program's by a relative error of at most 0.008.
Values may be sent and summed in bfloat16 or wider, within the bound.
No kernel may reach another device: no remote copies, remote signals or barrier semaphores. Data moves between devices by JAX's collectives and lax.ppermute only.
A program may use at most 64 MiB of HBM per device.

v0:
```python
import math
import jax
import jax.numpy as jnp
from jax import lax
from jax.sharding import PartitionSpec as P

TAPS = 3
BLK = 8


def from_behind(shard, axis, by):
    count = lax.axis_size(axis)
    pairs = [(i, i + by) for i in range(count) if 0 <= i + by < count]
    return lax.ppermute(shard, axis, pairs)


def exact_dot(pattern, matrix, tensor):
    return jnp.einsum(pattern, matrix, tensor, precision=lax.Precision.HIGHEST)


def turn_angles(numbers, period):
    return (numbers % period).astype(jnp.float32) * (2.0 * math.pi / period)


def ring_body(fresh, library, block_slot, prefix_blocks, short_taps, long_filter, skip_gain):
    row_count = fresh.shape[0]
    channels = fresh.shape[2]
    devices = lax.axis_size("seq")
    seq_index = lax.axis_index("seq")
    group_rows = row_count // devices
    period = 2 * row_count * devices
    block_ids = jnp.arange(devices, dtype=jnp.int32)
    mode_ids = jnp.arange(2 * devices, dtype=jnp.int32)
    coarse = turn_angles(mode_ids[:, None] * block_ids[None, :], 2 * devices)
    cos_q = jnp.cos(coarse)
    sin_q = jnp.sin(coarse)
    local_rows = seq_index * group_rows + jnp.arange(group_rows, dtype=jnp.int32)
    twist = turn_angles(mode_ids[:, None] * local_rows[None, :], period)
    twist_cos = jnp.cos(twist)[:, :, None]
    twist_sin = jnp.sin(twist)[:, :, None]
    row_ids = jnp.arange(row_count, dtype=jnp.int32)
    fine_angles = turn_angles(row_ids[:, None] * row_ids[None, :], row_count)
    cos_m = jnp.cos(fine_angles)
    sin_m = jnp.sin(fine_angles)
    first_modes = 2 * seq_index + jnp.arange(2, dtype=jnp.int32)
    back_twist = turn_angles(first_modes[:, None] * row_ids[None, :], period)
    back_cos = jnp.cos(back_twist)[:, :, None]
    back_sin = jnp.sin(back_twist)[:, :, None]

    def to_modes(column):
        real_part = exact_dot("kq,qgc->kgc", cos_q, column)
        imag_part = -exact_dot("kq,qgc->kgc", sin_q, column)
        return jnp.stack(
            [
                real_part * twist_cos + imag_part * twist_sin,
                imag_part * twist_cos - real_part * twist_sin,
            ]
        )

    def to_spectrum(spread):
        real_part = exact_dot("ki,jic->jkc", cos_m, spread[0]) + exact_dot(
            "ki,jic->jkc", sin_m, spread[1]
        )
        imag_part = exact_dot("ki,jic->jkc", cos_m, spread[1]) - exact_dot(
            "ki,jic->jkc", sin_m, spread[0]
        )
        return (real_part, imag_part)

    blocks_here = row_count // BLK
    flat_ids = prefix_blocks.reshape(-1)
    first_block = jnp.minimum(seq_index * blocks_here, flat_ids.shape[0] - blocks_here)
    own_ids = lax.dynamic_slice_in_dim(flat_ids, first_block, blocks_here)
    matches = own_ids[:, None] == jnp.arange(block_slot.shape[0], dtype=jnp.int32)[None, :]
    wanted = jnp.sum(jnp.where(matches, block_slot[None, :], 0), axis=1)
    shards = lax.all_gather(library, "seq", axis=0, tiled=True)
    picker = (wanted[:, None] == jnp.arange(shards.shape[0], dtype=jnp.int32)[None, :]).astype(
        jnp.bfloat16
    )
    gathered = jnp.einsum("bn,nlc->blc", picker, shards, preferred_element_type=jnp.float32)
    cached = gathered.reshape(row_count, channels).astype(jnp.bfloat16)
    values = jnp.where(seq_index < devices // 4, cached, fresh[:, 2])
    stacked = jnp.concatenate([fresh[:, :2], values[:, None]], axis=1)
    previous = from_behind(stacked[row_count - (TAPS - 1) :], "seq", 1)
    extended = jnp.concatenate([previous, stacked], axis=0)
    shortened = jnp.zeros((row_count, 3, channels), jnp.float32)
    for offset in range(TAPS):
        window_start = TAPS - 1 - offset
        shortened = shortened + short_taps[offset][None] * extended[
            window_start : window_start + row_count
        ].astype(jnp.float32)
    gating = shortened[:, 0]
    signal = shortened[:, 1] * shortened[:, 2]
    spread_signal = to_modes(
        lax.all_to_all(signal[None], "seq", split_axis=1, concat_axis=0, tiled=True)
    )
    spread_taps = to_modes(
        lax.all_to_all(long_filter[None], "seq", split_axis=1, concat_axis=0, tiled=True)
    )
    moved_signal, moved_taps = (
        lax.all_to_all(
            spread_signal.astype(jnp.bfloat16), "seq", split_axis=1, concat_axis=2, tiled=True
        ).astype(spread_signal.dtype),
        lax.all_to_all(
            spread_taps.astype(jnp.bfloat16), "seq", split_axis=1, concat_axis=2, tiled=True
        ).astype(spread_taps.dtype),
    )
    sig_real, sig_imag = to_spectrum(moved_signal)
    tap_real, tap_imag = to_spectrum(moved_taps)
    prod_real = sig_real * tap_real - sig_imag * tap_imag
    prod_imag = sig_real * tap_imag + sig_imag * tap_real
    back_real = exact_dot("ki,jic->jkc", cos_m, prod_real) - exact_dot(
        "ki,jic->jkc", sin_m, prod_imag
    )
    back_imag = exact_dot("ki,jic->jkc", cos_m, prod_imag) + exact_dot(
        "ki,jic->jkc", sin_m, prod_real
    )
    turned = jnp.stack(
        [back_real * back_cos - back_imag * back_sin, back_imag * back_cos + back_real * back_sin]
    )
    spread = lax.all_to_all(turned, "seq", split_axis=2, concat_axis=1, tiled=True)
    positions = (
        exact_dot("kq,kgc->qgc", cos_q, spread[0]) - exact_dot("kq,kgc->qgc", sin_q, spread[1])
    ) / period
    convolved = lax.all_to_all(positions, "seq", split_axis=0, concat_axis=1, tiled=True)[0]
    output = gating * (convolved + skip_gain[None, :] * signal)
    return output.astype(jnp.bfloat16)


def dft_tables(tokens):
    period = 2 * tokens
    width = 1
    while width * width < tokens:
        width *= 2
    outer = tokens // width
    freqs = jnp.arange(tokens + 1, dtype=jnp.int32)[:, None]
    coarse = turn_angles(freqs * (width * jnp.arange(outer, dtype=jnp.int32))[None, :], period)
    fine = turn_angles(freqs * jnp.arange(width, dtype=jnp.int32)[None, :], period)
    c1, s1 = (jnp.cos(coarse)[:, :, None], jnp.sin(coarse)[:, :, None])
    c2, s2 = (jnp.cos(fine)[:, None, :], jnp.sin(fine)[:, None, :])
    cos_t = (c1 * c2 - s1 * s2).reshape(tokens + 1, tokens)
    sin_t = (s1 * c2 + c1 * s2).reshape(tokens + 1, tokens)
    return (cos_t, sin_t)


def local_body(fresh, library, block_slot, prefix_blocks, short_taps, long_filter, skip_gain):
    row_count, _, channels = fresh.shape
    devices = lax.axis_size("seq")
    seq_index = lax.axis_index("seq")
    tokens = row_count * devices
    own = channels // devices
    lib_here = library.shape[0]
    lib_rows = lib_here * BLK // 4
    packed = jnp.concatenate([fresh, long_filter.astype(jnp.bfloat16)[:, None, :]], axis=1)
    packed = jnp.concatenate([packed, library.reshape(lib_rows, 4, channels)], axis=0)
    moved = lax.all_to_all(packed, "seq", split_axis=2, concat_axis=0, tiled=True)
    moved = moved.reshape(devices, row_count + lib_rows, 4, own)
    rows = moved[:, :row_count].reshape(tokens, 4, own)
    lib_all = moved[:, row_count:].reshape(devices * lib_here, BLK * own)
    slot_ids = block_slot[prefix_blocks.reshape(-1)]
    prefix_len = slot_ids.shape[0] * BLK
    picker = (slot_ids[:, None] == jnp.arange(lib_all.shape[0], dtype=jnp.int32)[None, :]).astype(
        jnp.bfloat16
    )
    cached = jnp.dot(picker, lib_all, preferred_element_type=jnp.float32)
    cached = cached.reshape(prefix_len, own).astype(jnp.bfloat16)
    values = jnp.concatenate([cached, rows[prefix_len:, 2]], axis=0)
    stacked = jnp.concatenate([rows[:, :2], values[:, None]], axis=1).astype(jnp.float32)
    taps = lax.dynamic_slice_in_dim(short_taps, seq_index * own, own, axis=2)
    gain = lax.dynamic_slice_in_dim(skip_gain, seq_index * own, own, axis=0)
    shortened = jnp.zeros((tokens, 3, own), jnp.float32)
    for offset in range(TAPS):
        shifted = jnp.pad(stacked[: tokens - offset], ((offset, 0), (0, 0), (0, 0)))
        shortened = shortened + taps[offset][None] * shifted
    gating = shortened[:, 0]
    signal = shortened[:, 1] * shortened[:, 2]
    cos_t, sin_t = dft_tables(tokens)
    table = jnp.concatenate([cos_t, sin_t], axis=0).astype(jnp.bfloat16)
    operands = jnp.concatenate([signal.astype(jnp.bfloat16), rows[:, 3]], axis=1)
    spec = jnp.dot(table, operands, preferred_element_type=jnp.float32)
    bins = tokens + 1
    sig_c, tap_c = (spec[:bins, :own], spec[:bins, own:])
    sig_s, tap_s = (spec[bins:, :own], spec[bins:, own:])
    weight = jnp.where((jnp.arange(bins) == 0) | (jnp.arange(bins) == tokens), 1.0, 2.0).astype(
        jnp.float32
    )[:, None] / (2 * tokens)
    real = (sig_c * tap_c - sig_s * tap_s) * weight
    turned = (sig_c * tap_s + sig_s * tap_c) * weight
    back = jnp.concatenate([real, turned], axis=0).astype(jnp.bfloat16)
    convolved = lax.dot_general(
        table, back, (((0,), (0,)), ((), ())), preferred_element_type=jnp.float32
    )
    output = (gating * (convolved + gain[None, :] * signal)).astype(jnp.bfloat16)
    return lax.all_to_all(output, "seq", split_axis=0, concat_axis=1, tiled=True)


def body(fresh, library, *rest):
    devices = lax.axis_size("seq")
    tokens = fresh.shape[0] * devices
    fits = tokens <= 4096 and fresh.shape[2] % devices == 0 and (library.shape[0] * BLK % 4 == 0)
    if fits:
        return local_body(fresh, library, *rest)
    return ring_body(fresh, library, *rest)


def solution(mesh):
    return jax.shard_map(
        body,
        mesh=mesh,
        in_specs=(
            P(("group", "seq"), None, "chan"),
            P("seq", None, "chan"),
            P(),
            P("group", None),
            P(None, None, "chan"),
            P("seq", "chan"),
            P("chan"),
        ),
        out_specs=P(("group", "seq"), "chan"),
        check_vma=False,
    )
```

profile of v0, /device:TPU:0, one launch (start us, length us, event | category | flops | bytes accessed | tf_op | source)
XLA Modules:
  0.0 86.8 jit_solution(6593084510004803457)
XLA Ops:
  0.0 0.0 copy-start
  0.0 0.8 reshape.169
  0.8 1.1 %convert_bitcast_fusion = bf16[128,1,1024]{2,0,1:T(8,128)(2,1)S(1)} fusion(f32[128,1024]{1,0:T(8,128)} %param.12), kind=kLoop, calls=%fused_computation.27 | loop fusion | flops 131072 | bytes 786432 | tf_op jit(solution)/shard_map/broadcast_in_dim | solution.py:153
  1.9 0.4 copy.37
  2.3 0.7 copy.38
  3.1 0.0 copy-done.3
  3.1 0.7 copy.36
  3.8 2.9 %pad_maximum_fusion.3 = bf16[130,4,1024]{0,1,2:T(4,128)(2,1)} fusion(bf16[2,4,1024]{0,1,2:T(4,128)(2,1)S(1)} %copy.38, bf16[128,1,1024]{0,1,2:T(2,128)(2,1)S(1)} %copy.37, bf16[128,3,1024]{0,1,2:T(4,128)(2,1)S(1)} %copy.36), kind=kLoop, calls=%fused_computation.6 | loop fusion | flops 3194880 | bytes 2129920 | tf_op jit(solution)/shard_map/concatenate | solution.py:154
  6.7 7.4 %all-to-all-start = ((bf16[130,4,1024]{0,1,2:T(4,128)(2,1)}), bf16[130,4,1024]{0,1,2:T(4,128)(2,1)S(1)}, u32[]{:S(2)}, u32[]{:S(2)}) async-start(bf16[130,4,1024]{0,1,2:T(4,128)(2,1)} %pad_maximum_fusion.3), calls=%async_computation | async-start | bytes 4194304 | tf_op jit(solution)/shard_map/all_to_all | solution.py:155
  14.1 0.1 copy.41
  14.2 0.1 reshape.171
  14.3 0.8 dynamic_slice.7
  15.0 0.7 gather_fusion
  15.7 0.7 dynamic-slice_bitcast_fusion.2
  16.5 0.6 fusion.25
  17.1 0.7 fusion.28
  17.7 3.7 %subtract_convert_fusion = (bf16[1025,32,32]{0,2,1:T(8,128)(2,1)}, bf16[1025,32,32]{0,2,1:T(8,128)(2,1)}) fusion(f32[1025,32]{0,1:T(8,128)S(1)} %get-tuple-element.14, f32[1025,32]{0,1:T(8,128)S(1)} %get-tuple-element.13, f32[1025,32]{0,1:T(8,128)S(1)} %get-tuple-element.15, f32[1025,32]{0,1:T(8,128)S(1)} %get-tuple-element.12), kind=kLoop, calls=%fused_computation.2 | loop fusion | flops 8396800 | bytes 4723200 | tf_op jit(solution)/shard_map/convert.5
  21.4 40.9 %all-to-all-done = bf16[130,4,1024]{0,1,2:T(4,128)(2,1)S(1)} async-done(((bf16[130,4,1024]{0,1,2:T(4,128)(2,1)}), bf16[130,4,1024]{0,1,2:T(4,128)(2,1)S(1)}, u32[]{:S(2)}, u32[]{:S(2)}) %all-to-all-start) | async-done | bytes 1064992 | tf_op jit(solution)/shard_map/all_to_all | solution.py:155
  62.3 3.9 %copy.43 = bf16[130,4,8,128]{3,2,1,0:T(8,128)(2,1)S(1)} copy(bf16[130,4,8,128]{0,1,3,2:T(4,128)(2,1)S(1)} %bitcast.44) | data formatting | bytes 2129920 | tf_op jit(solution)/shard_map/all_to_all | solution.py:155
  66.3 0.1 slice.70
  66.3 0.4 copy.40
  66.8 0.2 convolution_convert_fusion
  67.1 0.1 maximum_convert_fusion
  67.2 0.5 multiply_add_fusion
  67.8 0.1 fusion.12
  67.9 1.0 %copy-done.1 = bf16[1025,32,32]{0,2,1:T(8,128)(2,1)S(1)} copy-done((bf16[1025,32,32]{0,2,1:T(8,128)(2,1)S(1)}, bf16[1025,32,32]{0,2,1:T(8,128)(2,1)}, u32[]{:S(2)}) %copy-start.1) | copy-done | bytes 2099224
  68.9 0.7 copy-done.2
  69.6 2.2 %fusion.1 = f32[2050,256]{1,0:T(8,128)S(1)} fusion(bf16[1025,1024]{0,1:T(8,128)(2,1)S(1)} %bitcast.52, bf16[1025,1024]{0,1:T(8,128)(2,1)S(1)} %bitcast.50, bf16[1024,128]{1,0:T(8,128)(2,1)S(1)} %slice_bitcast_fusion.1, bf16[1024,128]{1,0:T(8,128)(2,1)S(1)} %fusion.12), kind=kOutput, calls=%fused_computation.5 | convolution fusion | flops 1084235776 | bytes 6821888 | tf_op jit(solution)/shard_map/dot_general | solution.py:179
  71.8 0.3 multiply_convert_fusion.1
  72.1 1.4 %fusion.4 = bf16[1024,128]{1,0:T(8,128)(2,1)S(1)} fusion(bf16[1025,1024]{0,1:T(8,128)(2,1)S(1)} %bitcast.53, bf16[1025,1024]{0,1:T(8,128)(2,1)S(1)} %bitcast.51, bf16[1025,128]{1,0:T(8,128)(2,1)S(1)} %get-tuple-element.6, bf16[1025,128]{1,0:T(8,128)(2,1)S(1)} %get-tuple-element.5, f32[1024,3,128]{2,0,1:T(8,128)S(1)} %multiply_add_fusion, ...), kind=kOutput, calls=%fused_computation.10 | convolution fusion | flops 547496960 | bytes 6558720 | tf_op jit(solution)/shard_map/dot_general | solution.py:189
  73.5 12.5 %all_to_all.34 = bf16[8,128,128]{2,1,0:T(8,128)(2,1)S(1)} all-to-all(bf16[8,128,128]{2,1,0:T(8,128)(2,1)S(1)} %bitcast.54), channel_id=1, replica_groups=mesh['group'=2,'seq'=8,'chan'=2] {'seq'}, dimensions={0} | all-to-all | bytes 524288 | tf_op jit(solution)/shard_map/all_to_all | solution.py:193
  86.0 0.7 copy_bitcast_fusion
  (16 shorter events, 0.2 us)
Async XLA Ops:
  0.0 15.0 %copy-start = (s32[8]{0:T(128)S(1)}, s32[8]{0:T(128)}, u32[]{:S(2)}) copy-start(s32[8]{0:T(128)} %param.9) | copy-start | bytes 100
  0.0 3.1 %copy-start.3 = (bf16[128,3,1024]{2,0,1:T(8,128)(2,1)S(1)}, bf16[128,3,1024]{2,0,1:T(8,128)(2,1)}, u32[]{:S(2)}) copy-start(bf16[128,3,1024]{2,0,1:T(8,128)(2,1)} %param.7) | copy-start | bytes 2359300
  6.7 7.4 %copy-start.4 = (s32[8,4]{0,1:T(4,128)S(1)}, s32[8,4]{0,1:T(4,128)}, u32[]{:S(2)}) copy-start(s32[8,4]{0,1:T(4,128)} %param.10) | copy-start | bytes 388
  6.7 55.7 %all-to-all-start = ((bf16[130,4,1024]{0,1,2:T(4,128)(2,1)}), bf16[130,4,1024]{0,1,2:T(4,128)(2,1)S(1)}, u32[]{:S(2)}, u32[]{:S(2)}) async-start(bf16[130,4,1024]{0,1,2:T(4,128)(2,1)} %pad_maximum_fusion.3), calls=%async_computation | async-start | bytes 4194304 | tf_op jit(solution)/shard_map/all_to_all | solution.py:155
  67.2 1.7 %copy-start.1 = (bf16[1025,32,32]{0,2,1:T(8,128)(2,1)S(1)}, bf16[1025,32,32]{0,2,1:T(8,128)(2,1)}, u32[]{:S(2)}) copy-start(bf16[1025,32,32]{0,2,1:T(8,128)(2,1)} %get-tuple-element.7) | copy-start | bytes 6297604
  67.2 2.4 %copy-start.2 = (bf16[1025,32,32]{0,2,1:T(8,128)(2,1)S(1)}, bf16[1025,32,32]{0,2,1:T(8,128)(2,1)}, u32[]{:S(2)}) copy-start(bf16[1025,32,32]{0,2,1:T(8,128)(2,1)} %get-tuple-element.8) | copy-start | bytes 6297604
where the time goes:
time: 87.2 us; the launch traced here: 86.8 us
  waiting for transfers between devices  40.9 us (47%)
  blocking collectives  12.5 us (14%)
  local copies, waits for them, and re-layouts  12 us (14%)
  other arithmetic  9.91 us (11%)
  starting transfers between devices  7.41 us (8%)
  matrix products  3.8 us (4%)
    all_to_all x1, waiting for transfers between devices, local_body(): lax.all_to_all(packed, 'seq', split_axis=2, concat_axis=0, tiled=True)  40.9 us
    all_to_all x1, blocking collectives, local_body(): lax.all_to_all(output, 'seq', split_axis=0, concat_axis=1, tiled=True)  12.5 us
    all_to_all x1, starting transfers between devices, local_body(): lax.all_to_all(packed, 'seq', split_axis=2, concat_axis=0, tiled=True)  7.41 us
    another operation x2, other arithmetic  3.99 us
    all_to_all x1, local copies, waits for them, and re-layouts, local_body(): lax.all_to_all(packed, 'seq', split_axis=2, concat_axis=0, tiled=True)  3.92 us
    concatenate x1, other arithmetic, local_body(): jnp.concatenate([packed, library.reshape(lib_rows, 4, channels)], axis=0)  2.86 us
    unnamed x12, local copies, waits for them, and re-layouts  2.58 us
    dot_general x1, matrix products, local_body(): spec = jnp.dot(table, operands, preferred_element_type=jnp.float32)  2.2 us
  transfers between devices with their start and end apart: 1, of which 1 were waited for; matrix products, arithmetic and copies ran while one was open for 8% of the time, Pallas kernels for 0%

commit v1 on v0

--- a/solution.py
+++ b/solution.py
@@ -152,7 +152,23 @@
     lib_rows = lib_here * BLK // 4
     packed = jnp.concatenate([fresh, long_filter.astype(jnp.bfloat16)[:, None, :]], axis=1)
     packed = jnp.concatenate([packed, library.reshape(lib_rows, 4, channels)], axis=0)
-    moved = lax.all_to_all(packed, "seq", split_axis=2, concat_axis=0, tiled=True)
+    carry_in = jax.lax.axis_size("seq")
+    big = jax.lax.axis_index("seq")
+    field_out, inter = (carry_in, big)
+    reached = packed.shape[2] // field_out
+    block_now = list(packed.shape)
+    block_now[2] = reached
+    r_now = block_now[0]
+    block_now[0] = r_now * field_out
+    moved = jnp.zeros(block_now, packed.dtype)
+    for ii in tuple(range(field_out)):
+        current_block = lax.dynamic_slice_in_dim(packed, (inter ^ ii) * reached, reached, axis=2)
+        if ii:
+            sheets = []
+            for pp in [*range(field_out)]:
+                sheets.append((pp, pp ^ ii))
+            current_block = jax.lax.ppermute(current_block, "seq", sheets)
+        moved = lax.dynamic_update_slice_in_dim(moved, current_block, (inter ^ ii) * r_now, axis=0)
     moved = moved.reshape(devices, row_count + lib_rows, 4, own)
     rows = moved[:, :row_count].reshape(tokens, 4, own)
     lib_all = moved[:, row_count:].reshape(devices * lib_here, BLK * own)

time: 87.2 us -> 57.5 us (0.66)
  waiting for transfers between devices: 40.9 us -> 5.67 us
  starting transfers between devices: 7.41 us -> 14.6 us
  other arithmetic: 9.91 us -> 8.22 us
  blocking collectives: 12.5 us -> 13.9 us
  local copies, waits for them, and re-layouts: 12 us -> 10.7 us
    all_to_all x1 -> x0, waiting for transfers between devices: 40.9 us -> none  [local_body(): lax.all_to_all(packed, 'seq', split_axis=2, concat_axis=0, tiled=True)]
    ppermute x0 -> x7, starting transfers between devices: none -> 14.6 us  [local_body(): current_block = jax.lax.ppermute(current_block, 'seq', sheets)]
    all_to_all x1 -> x0, starting transfers between devices: 7.41 us -> none  [local_body(): lax.all_to_all(packed, 'seq', split_axis=2, concat_axis=0, tiled=True)]
    ppermute x0 -> x7, waiting for transfers between devices: none -> 5.67 us  [local_body(): current_block = jax.lax.ppermute(current_block, 'seq', sheets)]
    dynamic_update_slice x0 -> x8, local copies, waits for them, and re-layouts: none -> 4.02 us  [local_body(): lax.dynamic_update_slice_in_dim(moved, current_block, (inter ^ ii) * r_no...]
    all_to_all x1 -> x0, local copies, waits for them, and re-layouts: 3.92 us -> none  [local_body(): lax.all_to_all(packed, 'seq', split_axis=2, concat_axis=0, tiled=True)]
    concatenate x1, other arithmetic: 2.86 us -> 1.24 us  [local_body(): jnp.concatenate([packed, library.reshape(lib_rows, 4, channels)], axis=0)]
    all_to_all x1, blocking collectives: 12.5 us -> 13.9 us  [local_body(): lax.all_to_all(output, 'seq', split_axis=0, concat_axis=1, tiled=True)]
  transfers between devices with their start and end apart: 1 -> 7, of which waited for: 1 -> 3; matrix products, arithmetic and copies ran while one was open for 8% -> 19% of each run, Pallas kernels for 0% -> 0%
where the time goes in v1:
time: 57.5 us; the launch traced here: 57.2 us
  starting transfers between devices  14.6 us (25%)
  blocking collectives  13.9 us (24%)
  local copies, waits for them, and re-layouts  10.7 us (19%)
  other arithmetic  8.22 us (14%)
  waiting for transfers between devices  5.67 us (10%)
  matrix products  3.79 us (7%)
    ppermute x7, starting transfers between devices, local_body(): current_block = jax.lax.ppermute(current_block, 'seq', sheets)  14.6 us
    all_to_all x1, blocking collectives, local_body(): lax.all_to_all(output, 'seq', split_axis=0, concat_axis=1, tiled=True)  13.9 us
    ppermute x7, waiting for transfers between devices, local_body(): current_block = jax.lax.ppermute(current_block, 'seq', sheets)  5.67 us
    dynamic_update_slice x8, local copies, waits for them, and re-layouts, local_body(): lax.dynamic_update_slice_in_dim(moved, current_block, (inter ^ ii) * r_no...  4.02 us
    another operation x2, other arithmetic  3.93 us
    dot_general x1, matrix products, local_body(): spec = jnp.dot(table, operands, preferred_element_type=jnp.float32)  2.19 us
    unnamed x9, local copies, waits for them, and re-layouts  1.85 us
    dot_general x1, matrix products, local_body(): lax.dot_general(table, back, (((0,), (0,)), ((), ())), preferred_element_...  1.39 us
  transfers between devices with their start and end apart: 7, of which 3 were waited for; matrix products, arithmetic and copies ran while one was open for 19% of the time, Pallas kernels for 0%

profile of v1, /device:TPU:0, one launch (start us, length us, event | category | flops | bytes accessed | tf_op | source)
XLA Modules:
  0.0 57.2 jit_solution(17596991148796696554)
XLA Ops:
  0.0 0.7 %reshape.170 = bf16[2,4,1024]{2,1,0:T(4,128)(2,1)S(1)} reshape(bf16[1,8,1024]{2,1,0:T(8,128)(2,1)} %param.8) | data formatting | bytes 32768 | tf_op jit(solution)/shard_map/reshape | solution.py:154
  0.8 1.1 %convert_bitcast_fusion = bf16[128,1,1024]{2,0,1:T(8,128)(2,1)S(1)} fusion(f32[128,1024]{1,0:T(8,128)} %param.12), kind=kLoop, calls=%fused_computation.27 | loop fusion | flops 131072 | bytes 786432 | tf_op jit(solution)/shard_map/broadcast_in_dim | solution.py:153
  1.9 1.2 %pad_maximum_fusion.9 = bf16[130,4,1024]{2,0,1:T(8,128)(2,1)S(1)} fusion(bf16[2,4,1024]{2,0,1:T(2,128)(2,1)S(1)} %copy.11, bf16[128,1,1024]{2,0,1:T(8,128)(2,1)S(1)} %convert_bitcast_fusion, bf16[128,3,1024]{2,0,1:T(8,128)(2,1)} %param.7), kind=kLoop, calls=%fused_computation.11 | loop fusion | flops 3194880 | bytes 2129920 | tf_op jit(solution)/shard_map/concatenate | solution.py:154
  3.5 6.1 %collective-permute-start.6 = (bf16[130,4,128]{2,0,1:T(8,128)(2,1)S(1)}, bf16[130,4,128]{2,0,1:T(8,128)(2,1)S(1)}, u32[]{:S(2)}, u32[]{:S(2)}) collective-permute-start(bf16[130,4,128]{2,0,1:T(8,128)(2,1)S(1)} %get-tuple-element.7), channel_id=1, source_target_pairs={{0,14},{2,12},{4,10},{6,8},{8,6},{10,4},{12,2},{14,0},{1,15},{3,13... | collective-permute-start | bytes 399368 | tf_op jit(solution)/shard_map/ppermute | solution.py:170
  9.8 0.8 %collective-permute-start.4 = (bf16[130,4,128]{2,0,1:T(8,128)(2,1)S(1)}, bf16[130,4,128]{2,0,1:T(8,128)(2,1)S(1)}, u32[]{:S(2)}, u32[]{:S(2)}) collective-permute-start(bf16[130,4,128]{2,0,1:T(8,128)(2,1)S(1)} %get-tuple-element.9), channel_id=1, source_target_pairs={{0,10},{2,8},{4,14},{6,12},{8,2},{10,0},{12,6},{14,4},{1,11},{3,9}... | collective-permute-start | bytes 399368 | tf_op jit(solution)/shard_map/ppermute | solution.py:170
  10.5 3.4 %collective-permute-start.1 = (bf16[130,4,128]{2,0,1:T(8,128)(2,1)S(1)}, bf16[130,4,128]{2,0,1:T(8,128)(2,1)S(1)}, u32[]{:S(2)}, u32[]{:S(2)}) collective-permute-start(bf16[130,4,128]{2,0,1:T(8,128)(2,1)S(1)} %get-tuple-element.12), channel_id=1, source_target_pairs={{0,4},{2,6},{4,0},{6,2},{8,12},{10,14},{12,8},{14,10},{1,5},{3,7},... | collective-permute-start | bytes 399368 | tf_op jit(solution)/shard_map/ppermute | solution.py:170
  13.9 1.5 %collective-permute-start = (bf16[130,4,128]{2,0,1:T(8,128)(2,1)S(1)}, bf16[130,4,128]{2,0,1:T(8,128)(2,1)S(1)}, u32[]{:S(2)}, u32[]{:S(2)}) collective-permute-start(bf16[130,4,128]{2,0,1:T(8,128)(2,1)S(1)} %get-tuple-element.13), channel_id=1, source_target_pairs={{0,2},{2,0},{4,6},{6,4},{8,10},{10,8},{12,14},{14,12},{1,3},{3,1},... | collective-permute-start | bytes 399368 | tf_op jit(solution)/shard_map/ppermute | solution.py:170
  15.4 0.6 %fusion.25 = (f32[1025,32]{0,1:T(8,128)S(1)}, f32[1025,32]{0,1:T(8,128)S(1)}) fusion(), kind=kLoop, calls=%fused_computation.48 | loop fusion | flops 459200 | bytes 262400 | tf_op jit(solution)/shard_map/sin | solution.py:139
  16.2 0.7 %fusion.28 = (f32[1025,32]{0,1:T(8,128)S(1)}, f32[1025,32]{0,1:T(8,128)S(1)}) fusion(s32[32]{0:T(128)S(1)} %iota_multiply_fusion), kind=kLoop, calls=%fused_computation.51 | loop fusion | flops 459200 | bytes 262528 | tf_op jit(solution)/shard_map/cos | solution.py:138
  16.8 3.7 %subtract_convert_fusion = (bf16[1025,32,32]{0,2,1:T(8,128)(2,1)}, bf16[1025,32,32]{0,2,1:T(8,128)(2,1)}) fusion(f32[1025,32]{0,1:T(8,128)S(1)} %get-tuple-element.22, f32[1025,32]{0,1:T(8,128)S(1)} %get-tuple-element.21, f32[1025,32]{0,1:T(8,128)S(1)} %get-tuple-element.23, f32[1025,32]{0,1:T(8,128)S(1)} %get-tuple-element.20), kind=kLoop, calls=%fused_computation.2 | loop fusion | flops 8396800 | bytes 4723200 | tf_op jit(solution)/shard_map/convert.5
  20.5 0.7 %fusion.32 = (f32[3,128]{1,0:T(4,128)S(1)}, f32[3,128]{1,0:T(4,128)S(1)}, f32[3,128]{1,0:T(4,128)S(1)}) fusion(f32[3,3,1024]{2,1,0:T(4,128)} %param.11, s32[]{:T(128)S(6)} %select_n.99, s32[]{:T(128)S(6)} %add.140, s32[]{:T(128)S(6)} %add.141), kind=kLoop, calls=%fused_computation.72 | loop fusion | bytes 9228 | tf_op jit(solution)/shard_map/mul | solution.py:189
  21.5 1.5 %collective-permute-start.3 = (bf16[130,4,128]{2,0,1:T(8,128)(2,1)S(1)}, bf16[130,4,128]{2,0,1:T(8,128)(2,1)S(1)}, u32[]{:S(2)}, u32[]{:S(2)}) collective-permute-start(bf16[130,4,128]{2,0,1:T(8,128)(2,1)S(1)} %get-tuple-element.10), channel_id=1, source_target_pairs={{0,8},{2,10},{4,12},{6,14},{8,0},{10,2},{12,4},{14,6},{1,9},{3,11}... | collective-permute-start | bytes 399368 | tf_op jit(solution)/shard_map/ppermute | solution.py:170
  23.0 1.2 %collective-permute-start.2 = (bf16[130,4,128]{2,0,1:T(8,128)(2,1)S(1)}, bf16[130,4,128]{2,0,1:T(8,128)(2,1)S(1)}, u32[]{:S(2)}, u32[]{:S(2)}) collective-permute-start(bf16[130,4,128]{2,0,1:T(8,128)(2,1)S(1)} %get-tuple-element.11), channel_id=1, source_target_pairs={{0,6},{2,4},{4,2},{6,0},{8,14},{10,12},{12,10},{14,8},{1,7},{3,5},... | collective-permute-start | bytes 399368 | tf_op jit(solution)/shard_map/ppermute | solution.py:170
  24.3 0.8 %dynamic_slice.39 = f32[128]{0:T(128)S(1)} dynamic-slice(f32[1024]{0:T(1024)} %param.13, s32[]{:T(128)S(6)} %select_n.99), dynamic_slice_sizes={128} | dynamic-slice | bytes 1028 | tf_op jit(solution)/shard_map/dynamic_slice | solution.py:185
  25.0 0.7 %gather_fusion = s32[32]{0:T(128)S(1)} fusion(s32[8]{0:T(128)S(1)} %copy-done, s32[1024]{0:T(1024)S(1)} %pad_clamp_fusion), kind=kCustom, calls=%fused_computation | custom fusion | bytes 384 | tf_op jit(solution)/shard_map/gather | solution.py:175
  25.9 0.5 dynamic_update_slice.24
  26.4 0.5 dynamic_update_slice.25
  26.9 0.5 dynamic_update_slice.26
  27.5 2.9 %collective-permute-done.2 = bf16[130,4,128]{2,0,1:T(8,128)(2,1)S(1)} collective-permute-done((bf16[130,4,128]{2,0,1:T(8,128)(2,1)S(1)}, bf16[130,4,128]{2,0,1:T(8,128)(2,1)S(1)}, u32[]{:S(2)}, u32[]{:S(2)}) %collective-permute-start.2) | collective-permute-done | bytes 133152 | tf_op jit(solution)/shard_map/ppermute | solution.py:170
  30.4 0.5 dynamic_update_slice.27
  30.9 2.4 %collective-permute-done.3 = bf16[130,4,128]{2,0,1:T(8,128)(2,1)S(1)} collective-permute-done((bf16[130,4,128]{2,0,1:T(8,128)(2,1)S(1)}, bf16[130,4,128]{2,0,1:T(8,128)(2,1)S(1)}, u32[]{:S(2)}, u32[]{:S(2)}) %collective-permute-start.3) | collective-permute-done | bytes 133152 | tf_op jit(solution)/shard_map/ppermute | solution.py:170
  33.3 0.5 dynamic_update_slice.28
  33.8 0.5 dynamic_update_slice.29
  34.4 0.5 dynamic_update_slice.30
  34.9 0.4 dynamic_update_slice.31
  36.3 0.5 multiply_add_fusion
  36.9 1.0 %copy-done.1 = bf16[1025,32,32]{0,2,1:T(8,128)(2,1)S(1)} copy-done((bf16[1025,32,32]{0,2,1:T(8,128)(2,1)S(1)}, bf16[1025,32,32]{0,2,1:T(8,128)(2,1)}, u32[]{:S(2)}) %copy-start.1) | copy-done | bytes 2099224
  38.0 0.7 %copy-done.2 = bf16[1025,32,32]{0,2,1:T(8,128)(2,1)S(1)} copy-done((bf16[1025,32,32]{0,2,1:T(8,128)(2,1)S(1)}, bf16[1025,32,32]{0,2,1:T(8,128)(2,1)}, u32[]{:S(2)}) %copy-start.2) | copy-done | bytes 2099224
  38.7 2.2 %fusion.1 = f32[2050,256]{1,0:T(8,128)S(1)} fusion(bf16[1025,1024]{0,1:T(8,128)(2,1)S(1)} %bitcast.49, bf16[1025,1024]{0,1:T(8,128)(2,1)S(1)} %bitcast.47, bf16[1024,128]{1,0:T(8,128)(2,1)S(1)} %slice_bitcast_fusion.1, bf16[1024,128]{1,0:T(8,128)(2,1)S(1)} %fusion.12), kind=kOutput, calls=%fused_computation.5 | convolution fusion | flops 1084235776 | bytes 6821888 | tf_op jit(solution)/shard_map/dot_general | solution.py:195
  41.2 1.4 %fusion.4 = bf16[1024,128]{1,0:T(8,128)(2,1)S(1)} fusion(bf16[1025,1024]{0,1:T(8,128)(2,1)S(1)} %bitcast.50, bf16[1025,1024]{0,1:T(8,128)(2,1)S(1)} %bitcast.48, bf16[1025,128]{1,0:T(8,128)(2,1)S(1)} %get-tuple-element.6, bf16[1025,128]{1,0:T(8,128)(2,1)S(1)} %get-tuple-element.5, f32[1024,3,128]{2,0,1:T(8,128)S(1)} %multiply_add_fusion, ...), kind=kOutput, calls=%fused_computation.9 | convolution fusion | flops 547496960 | bytes 6558720 | tf_op jit(solution)/shard_map/dot_general | solution.py:205
  42.6 13.9 %all_to_all.19 = bf16[8,128,128]{2,1,0:T(8,128)(2,1)S(1)} all-to-all(bf16[8,128,128]{2,1,0:T(8,128)(2,1)S(1)} %bitcast.51), channel_id=1, replica_groups=mesh['group'=2,'seq'=8,'chan'=2] {'seq'}, dimensions={0} | all-to-all | bytes 524288 | tf_op jit(solution)/shard_map/all_to_all | solution.py:209
  56.4 0.7 %copy_bitcast_fusion = bf16[128,1024]{1,0:T(8,128)(2,1)} fusion(bf16[8,128,128]{2,1,0:T(8,128)(2,1)S(1)} %all_to_all.19), kind=kLoop, calls=%fused_computation.24 | loop fusion | bytes 524288 | tf_op jit(solution)/shard_map/all_to_all | solution.py:209
  (34 shorter events, 2.4 us)
Async XLA Ops:
  0.0 25.0 %copy-start = (s32[8]{0:T(128)S(1)}, s32[8]{0:T(128)}, u32[]{:S(2)}) copy-start(s32[8]{0:T(128)} %param.9) | copy-start | bytes 100
  1.9 14.1 %copy-start.3 = (s32[8,4]{0,1:T(4,128)S(1)}, s32[8,4]{0,1:T(4,128)}, u32[]{:S(2)}) copy-start(s32[8,4]{0,1:T(4,128)} %param.10) | copy-start | bytes 388
  3.5 31.4 %collective-permute-start.6 = (bf16[130,4,128]{2,0,1:T(8,128)(2,1)S(1)}, bf16[130,4,128]{2,0,1:T(8,128)(2,1)S(1)}, u32[]{:S(2)}, u32[]{:S(2)}) collective-permute-start(bf16[130,4,128]{2,0,1:T(8,128)(2,1)S(1)} %get-tuple-element.7), channel_id=1, source_target_pairs={{0,14},{2,12},{4,10},{6,8},{8,6},{10,4},{12,2},{14,0},{1,15},{3,13... | collective-permute-start | bytes 399368 | tf_op jit(solution)/shard_map/ppermute | solution.py:170
  9.5 24.8 %collective-permute-start.5 = (bf16[130,4,128]{2,0,1:T(8,128)(2,1)S(1)}, bf16[130,4,128]{2,0,1:T(8,128)(2,1)S(1)}, u32[]{:S(2)}, u32[]{:S(2)}) collective-permute-start(bf16[130,4,128]{2,0,1:T(8,128)(2,1)S(1)} %get-tuple-element.8), channel_id=1, source_target_pairs={{0,12},{2,14},{4,8},{6,10},{8,4},{10,6},{12,0},{14,2},{1,13},{3,15... | collective-permute-start | bytes 399368 | tf_op jit(solution)/shard_map/ppermute | solution.py:170
  9.8 24.0 %collective-permute-start.4 = (bf16[130,4,128]{2,0,1:T(8,128)(2,1)S(1)}, bf16[130,4,128]{2,0,1:T(8,128)(2,1)S(1)}, u32[]{:S(2)}, u32[]{:S(2)}) collective-permute-start(bf16[130,4,128]{2,0,1:T(8,128)(2,1)S(1)} %get-tuple-element.9), channel_id=1, source_target_pairs={{0,10},{2,8},{4,14},{6,12},{8,2},{10,0},{12,6},{14,4},{1,11},{3,9}... | collective-permute-start | bytes 399368 | tf_op jit(solution)/shard_map/ppermute | solution.py:170
  10.5 11.0 %collective-permute-start.1 = (bf16[130,4,128]{2,0,1:T(8,128)(2,1)S(1)}, bf16[130,4,128]{2,0,1:T(8,128)(2,1)S(1)}, u32[]{:S(2)}, u32[]{:S(2)}) collective-permute-start(bf16[130,4,128]{2,0,1:T(8,128)(2,1)S(1)} %get-tuple-element.12), channel_id=1, source_target_pairs={{0,4},{2,6},{4,0},{6,2},{8,12},{10,14},{12,8},{14,10},{1,5},{3,7},... | collective-permute-start | bytes 399368 | tf_op jit(solution)/shard_map/ppermute | solution.py:170
  13.9 9.1 %collective-permute-start = (bf16[130,4,128]{2,0,1:T(8,128)(2,1)S(1)}, bf16[130,4,128]{2,0,1:T(8,128)(2,1)S(1)}, u32[]{:S(2)}, u32[]{:S(2)}) collective-permute-start(bf16[130,4,128]{2,0,1:T(8,128)(2,1)S(1)} %get-tuple-element.13), channel_id=1, source_target_pairs={{0,2},{2,0},{4,6},{6,4},{8,10},{10,8},{12,14},{14,12},{1,3},{3,1},... | collective-permute-start | bytes 399368 | tf_op jit(solution)/shard_map/ppermute | solution.py:170
  21.5 11.8 %collective-permute-start.3 = (bf16[130,4,128]{2,0,1:T(8,128)(2,1)S(1)}, bf16[130,4,128]{2,0,1:T(8,128)(2,1)S(1)}, u32[]{:S(2)}, u32[]{:S(2)}) collective-permute-start(bf16[130,4,128]{2,0,1:T(8,128)(2,1)S(1)} %get-tuple-element.10), channel_id=1, source_target_pairs={{0,8},{2,10},{4,12},{6,14},{8,0},{10,2},{12,4},{14,6},{1,9},{3,11}... | collective-permute-start | bytes 399368 | tf_op jit(solution)/shard_map/ppermute | solution.py:170
  23.0 7.4 %collective-permute-start.2 = (bf16[130,4,128]{2,0,1:T(8,128)(2,1)S(1)}, bf16[130,4,128]{2,0,1:T(8,128)(2,1)S(1)}, u32[]{:S(2)}, u32[]{:S(2)}) collective-permute-start(bf16[130,4,128]{2,0,1:T(8,128)(2,1)S(1)} %get-tuple-element.11), channel_id=1, source_target_pairs={{0,6},{2,4},{4,2},{6,0},{8,14},{10,12},{12,10},{14,8},{1,7},{3,5},... | collective-permute-start | bytes 399368 | tf_op jit(solution)/shard_map/ppermute | solution.py:170
  36.3 1.7 %copy-start.1 = (bf16[1025,32,32]{0,2,1:T(8,128)(2,1)S(1)}, bf16[1025,32,32]{0,2,1:T(8,128)(2,1)}, u32[]{:S(2)}) copy-start(bf16[1025,32,32]{0,2,1:T(8,128)(2,1)} %get-tuple-element.15) | copy-start | bytes 6297604
  36.3 2.4 %copy-start.2 = (bf16[1025,32,32]{0,2,1:T(8,128)(2,1)S(1)}, bf16[1025,32,32]{0,2,1:T(8,128)(2,1)}, u32[]{:S(2)}) copy-start(bf16[1025,32,32]{0,2,1:T(8,128)(2,1)} %get-tuple-element.16) | copy-start | bytes 6297604
